TPU v7x, 256 devices: a whole 4x4x8 slice. The times are simulated.
256 devices in a mesh: dp: 4 (over y_lo, core), row: 8 (over y_hi, x), col: 8 (over z).
Axes of the slice: x: 4, y: 4 (y_hi: 2, y_lo: 2; y = y_hi * 2 + y_lo), z: 8, core: 2. Of those that a mesh axis runs over, the one named last changes fastest.
Arguments:
- tokens: bfloat16 [3072, 4096], P('dp', ('row', 'col')), may hold values from -6 to 6
- cotangent: bfloat16 [3072, 4096], P('dp', ('row', 'col')), may hold values from -4 to 4
- gate_weight: bfloat16 [4096, 14336], P('row', 'col'), may hold values from -0.09375 to 0.09375
- up_weight: bfloat16 [4096, 14336], P('row', 'col'), may hold values from -0.09375 to 0.09375
- down_weight: bfloat16 [14336, 4096], P('col', 'row'), may hold values from -0.046875 to 0.046875
Outputs:
- layer_out: bfloat16 [3072, 4096], P(('dp', 'col'), 'row')
- input_grad: bfloat16 [3072, 4096], P(('dp', 'col'), 'row')
- gate_wgrad: bfloat16 [4096, 14336], P('row', 'col')
- up_wgrad: bfloat16 [4096, 14336], P('row', 'col')
- down_wgrad: bfloat16 [14336, 4096], P('col', 'row')
All inputs are finite; a program needn't handle non-finite values.
Results may differ from a plain program's by a relative error of at most 0.034.
Values may be sent and summed in bfloat16 or wider, within the bound.
No kernel may reach another device: no remote copies, remote signals or barrier semaphores. Data moves between devices by JAX's collectives and lax.ppermute only.
A program may use at most 128 MiB of HBM per device.

v0:
```python
import jax
import jax.numpy as jnp
from jax import lax
from jax.sharding import PartitionSpec as P


def contract_rows(left, right):
    return lax.dot_general(
        left, right, (((0,), (0,)), ((), ())), preferred_element_type=jnp.float32
    )


def contract_cols(left, right):
    return lax.dot_general(
        left, right, (((1,), (1,)), ((), ())), preferred_element_type=jnp.float32
    )


def local(tokens, cotangent, gate_weight, up_weight, down_weight):
    f32 = jnp.float32
    whole_x, whole_dy = (
        lax.all_gather(tokens, "col", axis=1, tiled=True),
        lax.all_gather(cotangent, "col", axis=1, tiled=True),
    )
    width = gate_weight.shape[1]
    rows = whole_x
    stacked = lax.psum_scatter(
        jnp.concatenate(
            [
                jnp.dot(rows, gate_weight, preferred_element_type=f32),
                jnp.dot(rows, up_weight, preferred_element_type=f32),
            ],
            axis=1,
        ).astype(jnp.bfloat16),
        "row",
        scatter_dimension=0,
        tiled=True,
    ).astype(jnp.float32)
    gate = stacked[:, :width]
    up = stacked[:, width:]
    sigma = jax.nn.sigmoid(gate)
    silu_gate = gate * sigma
    hidden = (silu_gate * up).astype(jnp.bfloat16)
    hidden_all = lax.all_gather(hidden, "row", axis=0, tiled=True)
    out_terms = jnp.dot(hidden_all, down_weight, preferred_element_type=f32)
    layer_out = lax.psum_scatter(
        out_terms.astype(jnp.bfloat16), "col", scatter_dimension=0, tiled=True
    )
    down_part = contract_rows(hidden_all, whole_dy).astype(jnp.bfloat16)
    rows = whole_dy
    hidden_grad = lax.psum_scatter(
        contract_cols(rows, down_weight).astype(jnp.bfloat16),
        "row",
        scatter_dimension=0,
        tiled=True,
    ).astype(jnp.float32)
    gate_grad = (hidden_grad * up * sigma * (1.0 + gate * (1.0 - sigma))).astype(jnp.bfloat16)
    up_grad = (hidden_grad * silu_gate).astype(jnp.bfloat16)
    gate_all, up_all = (
        lax.all_gather(gate_grad, "row", axis=0, tiled=True),
        lax.all_gather(up_grad, "row", axis=0, tiled=True),
    )
    input_grad = lax.psum_scatter(
        (contract_cols(gate_all, gate_weight) + contract_cols(up_all, up_weight)).astype(
            jnp.bfloat16
        ),
        "col",
        scatter_dimension=0,
        tiled=True,
    )
    gate_part = contract_rows(whole_x, gate_all).astype(jnp.bfloat16)
    up_part = contract_rows(whole_x, up_all).astype(jnp.bfloat16)
    gate_sum, up_sum, down_sum = (
        lax.psum(gate_part.astype(f32).astype(jnp.bfloat16), "dp").astype(jnp.float32),
        lax.psum(up_part.astype(f32).astype(jnp.bfloat16), "dp").astype(jnp.float32),
        lax.psum(down_part.astype(f32).astype(jnp.bfloat16), "dp").astype(jnp.float32),
    )
    gate_wgrad = gate_sum.astype(jnp.bfloat16)
    up_wgrad = up_sum.astype(jnp.bfloat16)
    down_wgrad = down_sum.astype(jnp.bfloat16)
    return (layer_out, input_grad, gate_wgrad, up_wgrad, down_wgrad)


def solution(mesh):
    in_specs = (
        P("dp", ("row", "col")),
        P("dp", ("row", "col")),
        P("row", "col"),
        P("row", "col"),
        P("col", "row"),
    )
    out_specs = (
        P(("dp", "col"), "row"),
        P(("dp", "col"), "row"),
        P("row", "col"),
        P("row", "col"),
        P("col", "row"),
    )
    return jax.shard_map(local, mesh=mesh, in_specs=in_specs, out_specs=out_specs, check_vma=False)
```

profile of v0, /device:TPU:2, one launch (start us, length us, event | category | flops | bytes accessed | tf_op | source)
XLA Modules:
  0.0 643.3 jit_solution(17645886271046592666)
XLA Ops:
  7.2 30.2 %all_gather.15 = bf16[768,512]{0,1:T(8,128)(2,1)S(1)} all-gather(bf16[768,64]{0,1:T(8,128)(2,1)} %param.5), channel_id=1, replica_groups=mesh['dp'=4,'row'=8,'col'=8] {'col'}, dimensions={1}, use_global_device_ids=true | all-gather | bytes 884736 | tf_op jit(solution)/shard_map/all_gather | solution.py:22
  37.4 3.5 convolution_convert_fusion.1
  40.9 1.6 convolution_convert_fusion.2
  42.5 2.8 pad_maximum_fusion
  46.2 26.1 %all_gather.17 = bf16[768,512]{0,1:T(8,128)(2,1)S(1)} all-gather(bf16[768,64]{0,1:T(8,128)(2,1)S(1)} %copy-done.4), channel_id=1, replica_groups=mesh['dp'=4,'row'=8,'col'=8] {'col'}, dimensions={1}, use_global_device_ids=true | all-gather | bytes 884736 | tf_op jit(solution)/shard_map/all_gather | solution.py:23
  73.2 3.2 convolution_convert_fusion
  76.5 66.3 %reduce-scatter.5.cloned.1.call-done = bf16[96,3584]{1,0:T(8,128)(2,1)} async-done(((bf16[768,3584]{1,0:T(8,128)(2,1)}), bf16[96,3584]{1,0:T(8,128)(2,1)}) %reduce-scatter.5.cloned.1.call-update) | async-done | bytes 688144 | tf_op jit(solution)/shard_map/reduce_scatter | solution.py:27
  144.0 86.2 %reduce-scatter.9.cloned.1.call-done = bf16[96,1792]{1,0:T(8,128)(2,1)} async-done(((bf16[768,1792]{1,0:T(8,128)(2,1)}), bf16[96,1792]{1,0:T(8,128)(2,1)}) %reduce-scatter.9.cloned.1.call-update) | async-done | bytes 344080 | tf_op jit(solution)/shard_map/reduce_scatter | solution.py:51
  230.1 2.3 fusion.5
  233.7 63.4 %all-gather.4.cloned.1.call-done = bf16[768,1792]{1,0:T(8,128)(2,1)} async-done(((bf16[96,1792]{1,0:T(8,128)(2,1)}), bf16[768,1792]{1,0:T(8,128)(2,1)}) %all-gather.4.cloned.1.call-update) | async-done | bytes 2752528 | tf_op jit(solution)/shard_map/all_gather | solution.py:44
  297.0 4.8 convolution_convert_fusion.3
  301.9 61.3 %all-gather.6.cloned.1.call-done = bf16[768,1792]{1,0:T(8,128)(2,1)} async-done(((bf16[96,1792]{1,0:T(8,128)(2,1)}), bf16[768,1792]{1,0:T(8,128)(2,1)}) %all-gather.6.cloned.1.call-update) | async-done | bytes 2752528 | tf_op jit(solution)/shard_map/all_gather | solution.py:60
  363.2 4.7 fusion
  367.9 61.5 %all-gather.8.cloned.1.call-done = bf16[768,1792]{1,0:T(8,128)(2,1)} async-done(((bf16[96,1792]{1,0:T(8,128)(2,1)}), bf16[768,1792]{1,0:T(8,128)(2,1)}) %all-gather.8.cloned.1.call-update) | async-done | bytes 2752528 | tf_op jit(solution)/shard_map/all_gather | solution.py:61
  429.4 4.7 fusion.1
  434.3 4.2 convolution_convert_fusion.6
  438.6 4.1 fusion.7
  442.7 2.5 add_convert_fusion
  445.3 105.7 %all-reduce.3.cloned.1.call-done = (bf16[512,1792]{0,1:T(8,128)(2,1)}, bf16[512,1792]{0,1:T(8,128)(2,1)}, bf16[1792,512]{1,0:T(8,128)(2,1)}) async-done(((bf16[512,1792]{0,1:T(8,128)(2,1)}, bf16[512,1792]{0,1:T(8,128)(2,1)}, bf16[1792,512]{1,0:T(8,128)(2,1)}), (bf16[512,1792]{0,1:T(8,128)(2,1)}, bf16[512,1792]{0,1:T(8,128)(2,1)}, bf16[1792,512]{1,0:T(8,128)(2,1)})) %all-reduce.3.cloned.1.call-update) | async-done | bytes 5505040 | tf_op jit(solution)/shard_map/psum | solution.py:74
  551.0 3.8 copy.10
  554.8 3.8 copy.11
  558.5 35.0 %reduce-scatter.7.cloned.1.call-done = bf16[96,512]{1,0:T(8,128)(2,1)} async-done(((bf16[768,512]{1,0:T(8,128)(2,1)}), bf16[96,512]{1,0:T(8,128)(2,1)}) %reduce-scatter.7.cloned.1.call-update) | async-done | bytes 98320 | tf_op jit(solution)/shard_map/reduce_scatter | solution.py:46
  593.5 40.1 %reduce-scatter.11.cloned.1.call-done = bf16[96,512]{1,0:T(8,128)(2,1)} async-done(((bf16[768,512]{1,0:T(8,128)(2,1)}), bf16[96,512]{1,0:T(8,128)(2,1)}) %reduce-scatter.11.cloned.1.call-update) | async-done | bytes 98320 | tf_op jit(solution)/shard_map/reduce_scatter | solution.py:63
  633.6 2.8 copy.15
  (33 shorter events, 4.6 us)
Async XLA Ops:
  7.2 66.1 %copy-start = (bf16[1792,512]{1,0:T(8,128)(2,1)S(1)}, bf16[1792,512]{1,0:T(8,128)(2,1)}, u32[]{:S(2)}) copy-start(bf16[1792,512]{1,0:T(8,128)(2,1)} %param.9) | copy-start | bytes 5505028
  7.2 135.6 %reduce-scatter.5.cloned.1.call-start = ((), (), s32[]{:S(2)}) async-start(), calls=%async_computation.4 | async-start | bytes 6193152 | tf_op jit(solution)/shard_map/reduce_scatter | solution.py:27
  37.4 3.5 copy-start.1
  37.4 3.5 copy-start.6
  45.3 0.9 copy-start.4
  45.4 184.8 %reduce-scatter.9.cloned.1.call-start = ((), (), s32[]{:S(2)}) async-start(), calls=%async_computation.7 | async-start | bytes 3096576 | tf_op jit(solution)/shard_map/reduce_scatter | solution.py:51
  72.4 0.9 copy-start.3
  76.4 220.6 %all-gather.4.cloned.1.call-start = ((), (), s32[]{:S(2)}) async-start(), calls=%async_computation.5 | async-start | bytes 3096576 | tf_op jit(solution)/shard_map/all_gather | solution.py:44
  232.4 130.8 %all-gather.6.cloned.1.call-start = ((), (), s32[]{:S(2)}) async-start(), calls=%async_computation.8 | async-start | bytes 3096576 | tf_op jit(solution)/shard_map/all_gather | solution.py:60
  233.0 196.4 %all-gather.8.cloned.1.call-start = ((), (), s32[]{:S(2)}) async-start(), calls=%async_computation.9 | async-start | bytes 3096576 | tf_op jit(solution)/shard_map/all_gather | solution.py:61
  233.6 129.6 %copy-start.2 = (bf16[768,512]{0,1:T(8,128)(2,1)S(1)}, bf16[768,512]{0,1:T(8,128)(2,1)}, u32[]{:S(2)}) copy-start(bf16[768,512]{0,1:T(8,128)(2,1)} %copy-done.1) | copy-start | bytes 2359300
  233.6 317.3 %all-reduce.3.cloned.1.call-start = ((), (), s32[]{:S(2)}) async-start(), calls=%async_computation.11 | async-start | bytes 11010048 | tf_op jit(solution)/shard_map/psum | solution.py:74
  434.1 159.4 %reduce-scatter.7.cloned.1.call-start = ((), (), s32[]{:S(2)}) async-start(), calls=%async_computation.6 | async-start | bytes 884736 | tf_op jit(solution)/shard_map/reduce_scatter | solution.py:46
  438.6 195.1 %reduce-scatter.11.cloned.1.call-start = ((), (), s32[]{:S(2)}) async-start(), calls=%async_computation.10 | async-start | bytes 884736 | tf_op jit(solution)/shard_map/reduce_scatter | solution.py:63
  438.6 4.1 copy-start.5
  438.6 4.1 copy-start.7
Sparse Core Ops, SparseCore 0:
  45.5 97.2 reduce-scatter.4
  146.9 83.1 reduce-scatter.8
  233.3 63.6 all-gather.3
  299.5 63.6 all-gather.5
  365.7 63.6 all-gather.7
  434.2 116.7 all-reduce.2
  554.1 39.4 reduce-scatter.6
  596.6 36.9 reduce-scatter.10
where the time goes:
time: 644 us; the launch traced here: 643 us
  waiting for transfers between devices  521 us (81%)
  blocking collectives  56.3 us (9%)
  matrix products  33.2 us (5%)
  between operations  14.2 us (2%)
  local copies, waits for them, and re-layouts  12.2 us (2%)
    psum x1, waiting for transfers between devices, local(): lax.psum(gate_part.astype(f32).astype(jnp.bfloat16), 'dp')  106 us
    reduce_scatter x1, waiting for transfers between devices, local(): lax.psum_scatter(contract_cols(rows, down_weight).astype(jnp.bfloat16), '...  86.2 us
    reduce_scatter x1, waiting for transfers between devices, local(): lax.psum_scatter(jnp.concatenate([jnp.dot(rows, gate_weight, preferred_el...  66.3 us
    all_gather x1, waiting for transfers between devices, local(): hidden_all = lax.all_gather(hidden, 'row', axis=0, tiled=True)  63.4 us
    all_gather x1, waiting for transfers between devices, local(): lax.all_gather(up_grad, 'row', axis=0, tiled=True)  61.5 us
    all_gather x1, waiting for transfers between devices, local(): lax.all_gather(gate_grad, 'row', axis=0, tiled=True)  61.3 us
    reduce_scatter x1, waiting for transfers between devices, local(): lax.psum_scatter((contract_cols(gate_all, gate_weight) + contract_cols(up...  40.1 us
    reduce_scatter x1, waiting for transfers between devices, local(): lax.psum_scatter(out_terms.astype(jnp.bfloat16), 'col', scatter_dimension...  35 us
  transfers between devices with their start and end apart: 8, of which 8 were waited for; matrix products, arithmetic and copies ran while one was open for 5% of the time, Pallas kernels for 0%

commit v1 on v0

--- a/solution.py
+++ b/solution.py
@@ -41,7 +41,9 @@
     sigma = jax.nn.sigmoid(gate)
     silu_gate = gate * sigma
     hidden = (silu_gate * up).astype(jnp.bfloat16)
-    hidden_all = lax.all_gather(hidden, "row", axis=0, tiled=True)
+    hidden_all = jnp.concatenate(
+        lax.all_to_all(jnp.stack([hidden] * lax.axis_size("row")), "row", 0, 0), axis=0
+    )
     out_terms = jnp.dot(hidden_all, down_weight, preferred_element_type=f32)
     layer_out = lax.psum_scatter(
         out_terms.astype(jnp.bfloat16), "col", scatter_dimension=0, tiled=True

time: 644 us -> 591 us (0.918)
  waiting for transfers between devices: 521 us -> 425 us
  blocking collectives: 56.3 us -> 98.7 us
    all_gather x1 -> x0, waiting for transfers between devices: 63.4 us -> none  [local(): hidden_all = lax.all_gather(hidden, 'row', axis=0, tiled=True)]
    all_to_all x0 -> x1, blocking collectives: none -> 42.5 us  [local(): lax.all_to_all(jnp.stack([hidden] * lax.axis_size('row')), 'row', 0, 0)]
    all_gather x1, waiting for transfers between devices: 61.3 us -> 30 us  [local(): lax.all_gather(gate_grad, 'row', axis=0, tiled=True)]
    unnamed x19 -> x23, local copies, waits for them, and re-layouts: 12.2 us -> 13.7 us
  transfers between devices with their start and end apart: 8 -> 7, of which waited for: 8 -> 7; matrix products, arithmetic and copies ran while one was open for 5% -> 5% of each run, Pallas kernels for 0% -> 0%
where the time goes in v1:
time: 591 us; the launch traced here: 590 us
  waiting for transfers between devices  425 us (72%)
  blocking collectives  98.7 us (17%)
  matrix products  31.3 us (5%)
  between operations  14.2 us (2%)
  local copies, waits for them, and re-layouts  13.9 us (2%)
  other arithmetic  6.31 us (1%)
    psum x1, waiting for transfers between devices, local(): lax.psum(gate_part.astype(f32).astype(jnp.bfloat16), 'dp')  106 us
    reduce_scatter x1, waiting for transfers between devices, local(): lax.psum_scatter(contract_cols(rows, down_weight).astype(jnp.bfloat16), '...  86.2 us
    reduce_scatter x1, waiting for transfers between devices, local(): lax.psum_scatter(jnp.concatenate([jnp.dot(rows, gate_weight, preferred_el...  66.6 us
    all_gather x1, waiting for transfers between devices, local(): lax.all_gather(up_grad, 'row', axis=0, tiled=True)  61.5 us
    all_to_all x1, blocking collectives, local(): lax.all_to_all(jnp.stack([hidden] * lax.axis_size('row')), 'row', 0, 0)  42.5 us
    reduce_scatter x1, waiting for transfers between devices, local(): lax.psum_scatter((contract_cols(gate_all, gate_weight) + contract_cols(up...  40.1 us
    reduce_scatter x1, waiting for transfers between devices, local(): lax.psum_scatter(out_terms.astype(jnp.bfloat16), 'col', scatter_dimension...  34.8 us
    all_gather x1, blocking collectives, local(): lax.all_gather(tokens, 'col', axis=1, tiled=True)  30.2 us
  transfers between devices with their start and end apart: 7, of which 7 were waited for; matrix products, arithmetic and copies ran while one was open for 5% of the time, Pallas kernels for 0%

profile of v1, /device:TPU:2, one launch (start us, length us, event | category | flops | bytes accessed | tf_op | source)
XLA Modules:
  0.0 590.5 jit_solution(7163894645758058857)
XLA Ops:
  7.2 30.2 %all_gather.12 = bf16[768,512]{0,1:T(8,128)(2,1)S(1)} all-gather(bf16[768,64]{0,1:T(8,128)(2,1)} %param.5), channel_id=1, replica_groups=mesh['dp'=4,'row'=8,'col'=8] {'col'}, dimensions={1}, use_global_device_ids=true | all-gather | bytes 884736 | tf_op jit(solution)/shard_map/all_gather | solution.py:22
  37.4 3.5 convolution_convert_fusion.1
  40.9 1.6 convolution_convert_fusion.2
  42.5 2.8 pad_maximum_fusion
  46.2 26.1 %all_gather.13 = bf16[768,512]{0,1:T(8,128)(2,1)S(1)} all-gather(bf16[768,64]{0,1:T(8,128)(2,1)S(1)} %copy-done.6), channel_id=1, replica_groups=mesh['dp'=4,'row'=8,'col'=8] {'col'}, dimensions={1}, use_global_device_ids=true | all-gather | bytes 884736 | tf_op jit(solution)/shard_map/all_gather | solution.py:23
  73.3 3.2 convolution_convert_fusion
  76.5 66.6 %reduce-scatter.5.cloned.1.call-done = bf16[96,3584]{1,0:T(8,128)(2,1)} async-done(((bf16[768,3584]{1,0:T(8,128)(2,1)}), bf16[96,3584]{1,0:T(8,128)(2,1)}) %reduce-scatter.5.cloned.1.call-update) | async-done | bytes 688144 | tf_op jit(solution)/shard_map/reduce_scatter | solution.py:27
  144.3 86.2 %reduce-scatter.9.cloned.1.call-done = bf16[96,1792]{1,0:T(8,128)(2,1)} async-done(((bf16[768,1792]{1,0:T(8,128)(2,1)}), bf16[96,1792]{1,0:T(8,128)(2,1)}) %reduce-scatter.9.cloned.1.call-update) | async-done | bytes 344080 | tf_op jit(solution)/shard_map/reduce_scatter | solution.py:53
  230.5 2.3 fusion.5
  233.6 42.5 %all_to_all.5 = bf16[8,96,1792]{2,1,0:T(8,128)(2,1)S(1)} all-to-all(bf16[8,96,1792]{2,1,0:T(8,128)(2,1)S(1)} %stack.2), channel_id=1, replica_groups=mesh['dp'=4,'row'=8,'col'=8] {'row'}, dimensions={0} | all-to-all | bytes 5505024 | tf_op jit(solution)/shard_map/all_to_all | solution.py:45
  277.6 2.9 convolution_convert_fusion.3
  280.5 30.0 %all-gather.3.cloned.1.call-done = bf16[768,1792]{1,0:T(8,128)(2,1)} async-done(((bf16[96,1792]{1,0:T(8,128)(2,1)}), bf16[768,1792]{1,0:T(8,128)(2,1)}) %all-gather.3.cloned.1.call-update) | async-done | bytes 2752528 | tf_op jit(solution)/shard_map/all_gather | solution.py:62
  310.5 4.7 fusion
  315.2 61.5 %all-gather.5.cloned.1.call-done = bf16[768,1792]{1,0:T(8,128)(2,1)} async-done(((bf16[96,1792]{1,0:T(8,128)(2,1)}), bf16[768,1792]{1,0:T(8,128)(2,1)}) %all-gather.5.cloned.1.call-update) | async-done | bytes 2752528 | tf_op jit(solution)/shard_map/all_gather | solution.py:63
  376.7 4.7 fusion.1
  381.6 4.2 convolution_convert_fusion.6
  386.0 4.1 fusion.7
  390.1 2.5 add_convert_fusion
  392.6 105.7 %all-reduce.3.cloned.1.call-done = (bf16[512,1792]{0,1:T(8,128)(2,1)}, bf16[512,1792]{0,1:T(8,128)(2,1)}, bf16[1792,512]{1,0:T(8,128)(2,1)}) async-done(((bf16[512,1792]{0,1:T(8,128)(2,1)}, bf16[512,1792]{0,1:T(8,128)(2,1)}, bf16[1792,512]{1,0:T(8,128)(2,1)}), (bf16[512,1792]{0,1:T(8,128)(2,1)}, bf16[512,1792]{0,1:T(8,128)(2,1)}, bf16[1792,512]{1,0:T(8,128)(2,1)})) %all-reduce.3.cloned.1.call-update) | async-done | bytes 5505040 | tf_op jit(solution)/shard_map/psum | solution.py:76
  498.3 3.8 copy.10
  502.1 3.8 copy.11
  505.9 34.8 %reduce-scatter.7.cloned.1.call-done = bf16[96,512]{1,0:T(8,128)(2,1)} async-done(((bf16[768,512]{1,0:T(8,128)(2,1)}), bf16[96,512]{1,0:T(8,128)(2,1)}) %reduce-scatter.7.cloned.1.call-update) | async-done | bytes 98320 | tf_op jit(solution)/shard_map/reduce_scatter | solution.py:48
  540.7 40.1 %reduce-scatter.11.cloned.1.call-done = bf16[96,512]{1,0:T(8,128)(2,1)} async-done(((bf16[768,512]{1,0:T(8,128)(2,1)}), bf16[96,512]{1,0:T(8,128)(2,1)}) %reduce-scatter.11.cloned.1.call-update) | async-done | bytes 98320 | tf_op jit(solution)/shard_map/reduce_scatter | solution.py:65
  580.8 2.8 copy.15
  (36 shorter events, 5.8 us)
Async XLA Ops:
  7.2 66.1 %copy-start = (bf16[1792,512]{1,0:T(8,128)(2,1)S(1)}, bf16[1792,512]{1,0:T(8,128)(2,1)}, u32[]{:S(2)}) copy-start(bf16[1792,512]{1,0:T(8,128)(2,1)} %param.9) | copy-start | bytes 5505028
  7.2 135.9 %reduce-scatter.5.cloned.1.call-start = ((), (), s32[]{:S(2)}) async-start(), calls=%async_computation.5 | async-start | bytes 6193152 | tf_op jit(solution)/shard_map/reduce_scatter | solution.py:27
  37.4 3.5 copy-start.2
  37.4 3.5 copy-start.8
  45.4 0.9 copy-start.6
  45.4 185.1 %reduce-scatter.9.cloned.1.call-start = ((), (), s32[]{:S(2)}) async-start(), calls=%async_computation.7 | async-start | bytes 3096576 | tf_op jit(solution)/shard_map/reduce_scatter | solution.py:53
  72.4 0.9 copy-start.4
  76.5 234.1 %all-gather.3.cloned.1.call-start = ((), (), s32[]{:S(2)}) async-start(), calls=%async_computation.8 | async-start | bytes 3096576 | tf_op jit(solution)/shard_map/all_gather | solution.py:62
  232.8 144.0 %all-gather.5.cloned.1.call-start = ((), (), s32[]{:S(2)}) async-start(), calls=%async_computation.9 | async-start | bytes 3096576 | tf_op jit(solution)/shard_map/all_gather | solution.py:63
  233.4 264.9 %all-reduce.3.cloned.1.call-start = ((), (), s32[]{:S(2)}) async-start(), calls=%async_computation.11 | async-start | bytes 11010048 | tf_op jit(solution)/shard_map/psum | solution.py:76
  233.6 44.0 %copy-start.5 = (bf16[768,512]{0,1:T(8,128)(2,1)S(1)}, bf16[768,512]{0,1:T(8,128)(2,1)}, u32[]{:S(2)}) copy-start(bf16[768,512]{0,1:T(8,128)(2,1)} %copy-done.4) | copy-start | bytes 2359300
  276.1 1.5 copy-start.1
  277.6 32.9 %copy-start.3 = (bf16[768,512]{0,1:T(8,128)(2,1)S(1)}, bf16[768,512]{0,1:T(8,128)(2,1)}, u32[]{:S(2)}) copy-start(bf16[768,512]{0,1:T(8,128)(2,1)} %copy-done.2) | copy-start | bytes 2359300
  381.4 159.3 %reduce-scatter.7.cloned.1.call-start = ((), (), s32[]{:S(2)}) async-start(), calls=%async_computation.6 | async-start | bytes 884736 | tf_op jit(solution)/shard_map/reduce_scatter | solution.py:48
  385.9 194.9 %reduce-scatter.11.cloned.1.call-start = ((), (), s32[]{:S(2)}) async-start(), calls=%async_computation.10 | async-start | bytes 884736 | tf_op jit(solution)/shard_map/reduce_scatter | solution.py:65
  385.9 4.1 copy-start.7
  386.0 4.1 copy-start.9
Sparse Core Ops, SparseCore 0:
  45.5 97.5 reduce-scatter.4
  147.2 83.2 reduce-scatter.8
  233.1 77.3 all-gather.2
  313.0 63.6 all-gather.4
  381.5 116.7 all-reduce.2
  501.2 39.4 reduce-scatter.6
  543.8 36.9 reduce-scatter.10
